TPU v7x, 256 devices: a whole 4x4x8 slice. The times are simulated.
256 devices in a mesh: gx: 32 (over z, x), gy: 8 (over y, core).
Axes of the slice: x: 4, y: 4, z: 8, core: 2. Of those that a mesh axis runs over, the one named last changes fastest.
Arguments:
- hidden_in: bfloat16 [64, 5120], P(None, 'gx'), may hold values from -60 to 60
- norm1_gain: float32 [5120], P('gx'), may hold values from 0.1 to 1.9
- norm1_bias: float32 [5120], P('gx'), may hold values from -4 to 4
- norm2_gain: float32 [5120], P('gx'), may hold values from 0.1 to 1.9
- norm2_bias: float32 [5120], P('gx'), may hold values from -4 to 4
- w_qkv: bfloat16 [5120, 15360], P('gx', 'gy'), may hold values from -0.078125 to 0.078125
- b_qkv: float32 [15360], P('gy'), may hold values from -4 to 4
- w_out: bfloat16 [5120, 5120], P('gy', 'gx'), may hold values from -0.078125 to 0.078125
- b_out: float32 [5120], P('gx'), may hold values from -4 to 4
- w_up: bfloat16 [5120, 20480], P('gx', 'gy'), may hold values from -0.078125 to 0.078125
- b_up: float32 [20480], P('gy'), may hold values from -4 to 4
- w_down: bfloat16 [20480, 5120], P('gy', 'gx'), may hold values from -0.0390625 to 0.0390625
- b_down: float32 [5120], P('gx'), may hold values from -4 to 4
- key_cache: bfloat16 [64, 40, 1024, 128], P('gx', 'gy'), may hold values from -70 to 70
- value_cache: bfloat16 [64, 40, 1024, 128], P('gx', 'gy'), may hold values from -6 to 6
- lengths: int32 [64], replicated, may hold values from 1 to 1024, 32768 in all
- assignment: int32 [64], replicated, may hold values from 0 to 63, each once
Outputs:
- hidden_out: bfloat16 [64, 5120], P(None, 'gx')
- new_keys: bfloat16 [64, 40, 1024, 128], P('gx', 'gy')
- new_values: bfloat16 [64, 40, 1024, 128], P('gx', 'gy')
Inputs may be any that keep to these rules, and one draw needn't show every extreme that they name: `lengths`: each request's length, the largest exactly 1024. `assignment`: a permutation: every slot holds exactly one request.
All inputs are finite; a program needn't handle non-finite values.
Results may differ from a plain program's by a relative error of at most 0.0068.
Values may be sent and summed in bfloat16 or wider, within the bound.
No kernel may reach another device: no remote copies, remote signals or barrier semaphores. Data moves between devices by JAX's collectives and lax.ppermute only.
A program may use at most 64 MiB of HBM per device.

v0:
```python
import jax
import jax.numpy as jnp
from jax import lax
from jax.sharding import PartitionSpec as P

D = 5120
HD = 128
ROT = 32


def rotate(tensor, position):
    half_rot = ROT // 2
    frequency = 10000.0 ** (-2.0 * jnp.arange(half_rot, dtype=jnp.float32) / ROT)
    angle = position.astype(jnp.float32)[:, None, None] * frequency
    cosine = jnp.cos(angle)
    sine = jnp.sin(angle)
    first_half = tensor[..., :half_rot]
    second_half = tensor[..., half_rot:ROT]
    return jnp.concatenate(
        [
            first_half * cosine - second_half * sine,
            second_half * cosine + first_half * sine,
            tensor[..., ROT:],
        ],
        axis=-1,
    )


def block_scores(query, keys, my_len):
    span_len = keys.shape[2]
    scores = jnp.einsum("shd,shpd->shp", query, keys, preferred_element_type=jnp.float32) * HD ** (
        -0.5
    )
    places = lax.iota(jnp.int32, span_len)
    valid = places[None, None, :] < my_len[:, None, None]
    return (jnp.where(valid, scores, -1e30), valid)


def on_device(
    hidden_in,
    norm1_gain,
    norm1_bias,
    norm2_gain,
    norm2_bias,
    w_qkv,
    b_qkv,
    w_out,
    b_out,
    w_up,
    b_up,
    w_down,
    b_down,
    key_cache,
    value_cache,
    lengths,
    assignment,
):
    requests = hidden_in.shape[0]
    rows_dev = key_cache.shape[0]
    heads_dev = key_cache.shape[1]
    wide_in = hidden_in.astype(jnp.float32)
    sum_rows, sum_squares = lax.psum(
        (jnp.sum(wide_in, axis=1), jnp.sum(wide_in * wide_in, axis=1)), "gx"
    )
    row_mean = sum_rows / D
    row_var = sum_squares / D - row_mean * row_mean
    normed = (wide_in - row_mean[:, None]) * lax.rsqrt(row_var + 1e-05)[:, None]
    attn_in = (normed * norm1_gain + norm1_bias).astype(jnp.bfloat16)
    mlp_in = (normed * norm2_gain + norm2_bias).astype(jnp.bfloat16)
    slot_ids = lax.iota(jnp.int32, requests)
    matches = assignment[:, None] == slot_ids[None, :]
    to_request = matches.astype(jnp.float32)
    attn_slot = jnp.dot(
        matches.T.astype(jnp.bfloat16), attn_in, preferred_element_type=jnp.float32
    ).astype(jnp.bfloat16)
    slot_len = jnp.sum(jnp.where(matches, lengths[:, None], 0), axis=0)
    my_len = lax.dynamic_slice_in_dim(slot_len, lax.axis_index("gx") * rows_dev, rows_dev, 0)
    qkv = (
        lax.psum_scatter(
            jnp.dot(attn_slot, w_qkv, preferred_element_type=jnp.float32),
            "gx",
            scatter_dimension=0,
            tiled=True,
        )
        + b_qkv
    )
    qkv = qkv.reshape(rows_dev, heads_dev, 3, HD)
    position = my_len - 1
    query = rotate(qkv[:, :, 0], position).astype(jnp.bfloat16)
    new_key = rotate(qkv[:, :, 1], position).astype(jnp.bfloat16)
    new_value = qkv[:, :, 2].astype(jnp.bfloat16)
    new_keys = key_cache
    new_values = value_cache
    zero_index = jnp.int32(0)
    for local_slot in range(rows_dev):
        slot_index = jnp.int32(local_slot)
        new_keys = lax.dynamic_update_slice(
            new_keys,
            new_key[local_slot][None, :, None, :],
            (slot_index, zero_index, position[local_slot], zero_index),
        )
        new_values = lax.dynamic_update_slice(
            new_values,
            new_value[local_slot][None, :, None, :],
            (slot_index, zero_index, position[local_slot], zero_index),
        )
    scores, valid = block_scores(query, new_keys, my_len)
    top_score = jnp.max(scores, axis=2)
    weights = jnp.where(valid, jnp.exp(scores - top_score[:, :, None]), 0.0)
    total = jnp.sum(weights, axis=2)
    weights_low = weights.astype(jnp.bfloat16)
    weighted = jnp.einsum(
        "shp,shpd->shd", weights_low, new_values, preferred_element_type=jnp.float32
    )
    attended = (weighted / total[:, :, None]).astype(jnp.bfloat16).reshape(rows_dev, heads_dev * HD)
    slot_part = jnp.dot(
        lax.all_gather(attended, "gx", axis=0, tiled=True),
        w_out,
        preferred_element_type=jnp.float32,
    )
    attn_part = jnp.dot(to_request, slot_part, precision=lax.Precision.HIGHEST)
    up_partial = jnp.dot(mlp_in, w_up, preferred_element_type=jnp.float32)
    up = lax.psum(up_partial, "gx") + b_up
    hidden = jax.nn.gelu(up, approximate=False).astype(jnp.bfloat16)
    mlp_part = jnp.dot(hidden, w_down, preferred_element_type=jnp.float32)
    branches = lax.psum(attn_part + mlp_part, "gy")
    hidden_out = (wide_in + branches + b_out + b_down).astype(jnp.bfloat16)
    return (hidden_out, new_keys, new_values)


def solution(mesh):
    return jax.shard_map(
        on_device,
        mesh=mesh,
        in_specs=(
            P(None, "gx"),
            P("gx"),
            P("gx"),
            P("gx"),
            P("gx"),
            P("gx", "gy"),
            P("gy"),
            P("gy", "gx"),
            P("gx"),
            P("gx", "gy"),
            P("gy"),
            P("gy", "gx"),
            P("gx"),
            P("gx", "gy", None, None),
            P("gx", "gy", None, None),
            P(),
            P(),
        ),
        out_specs=(P(None, "gx"), P("gx", "gy", None, None), P("gx", "gy", None, None)),
        check_vma=False,
    )
```

profile of v0, /device:TPU:2, one launch (start us, length us, event | category | flops | bytes accessed | tf_op | source)
XLA Modules:
  0.0 324.9 jit_solution(3638242814341928627)
XLA Ops:
  7.2 0.0 copy-start
  7.2 0.0 copy-start.3
  7.2 0.0 all-reduce.5.cloned.1.call-start
  7.2 1.8 copy-done.3
  9.0 0.0 copy-start.4
  9.0 0.0 copy-start.7
  9.0 0.0 copy-start.8
  9.0 0.0 copy-start.6
  9.0 0.0 copy-start.9
  9.0 0.0 copy-start.10
  9.0 1.5 copy.66
  10.5 0.0 copy-done.4
  10.5 0.0 copy-start.13
  10.5 0.0 copy-start.14
  10.5 0.1 convert_reduce_fusion
  10.7 73.7 %all-reduce.1 = (f32[64]{0:T(128)S(1)}, f32[64]{0:T(128)S(1)}) all-reduce(f32[64]{0:T(128)S(1)} %get-tuple-element.4, f32[64]{0:T(128)S(1)} %get-tuple-element.3), channel_id=1, replica_groups=mesh['gx'=32,'gy'=8] {'gx'}, use_global_device_ids=true, to_apply=%region_4.5 | all-reduce | flops 128 | bytes 1024 | tf_op jit(solution)/shard_map/psum | solution.py:62
  84.4 0.0 copy-done
  84.4 0.0 copy-done.7
  84.4 0.0 copy-done.8
  84.4 1.2 fusion.61
  85.5 0.0 copy-done.6
  85.5 0.0 copy-done.9
  85.5 0.0 copy-done.10
  85.5 2.5 fusion.4
  88.0 0.0 all-reduce.5.cloned.1.call-update
  88.1 0.0 copy-done.13
  88.1 0.1 select_reduce_fusion
  88.2 0.1 fusion.118
  88.3 0.6 fusion.122
  91.5 0.0 copy-done.14
  91.5 0.6 dynamic-slice
  94.1 0.1 multiply_cosine_fusion
  94.2 0.1 iota_compare_fusion.4
  94.3 142.2 %all-reduce.5.cloned.1.call-done = (f32[64,1920]{1,0:T(8,128)}, f32[64,2560]{1,0:T(8,128)}) async-done(((f32[64,1920]{1,0:T(8,128)}, f32[64,2560]{1,0:T(8,128)}), (f32[64,1920]{1,0:T(8,128)}, f32[64,2560]{1,0:T(8,128)})) %all-reduce.5.cloned.1.call-update) | async-done | bytes 1146896
  236.5 0.0 copy-done.5
  236.5 0.8 dynamic-slice_add_fusion
  237.4 0.1 slice.90
  237.5 0.1 slice.91
  237.5 0.1 subtract_convert_fusion.1
  237.6 0.1 pad_maximum_fusion
  237.7 1.3 dynamic_update_slice.12
  239.1 0.1 maximum_bitcast_fusion
  239.1 1.3 dynamic_update_slice.13
  240.5 2.5 fusion.84
  243.0 0.1 fusion.3
  243.1 0.1 fusion.119
  243.2 0.1 copy.42
  243.3 0.0 copy-done.2
  243.4 0.0 copy-start.1
  243.4 0.4 fusion.59
  243.8 0.1 fusion.83
  243.9 0.9 reshape.113
  244.8 41.8 %all-gather = bf16[32,2,640]{2,1,0:T(2,128)(2,1)S(1)} all-gather(bf16[1,2,640]{2,1,0:T(2,128)(2,1)} %reshape.113), channel_id=1, replica_groups=mesh['gx'=32,'gy'=8] {'gx'}, dimensions={0}, use_global_device_ids=true | all-gather | bytes 84480 | tf_op jit(solution)/shard_map/all_gather | solution.py:117
  286.6 0.7 reshape.114
  287.3 1.1 fusion.123
  288.5 0.9 fusion.77
  289.3 0.0 copy-start.11
  289.4 0.0 copy-start.12
  289.4 3.5 %convolution_add_fusion = f32[64,160]{1,0:T(8,128)} fusion(f32[64,160]{1,0:T(8,128)S(1)} %fusion.77, bf16[2560,160]{0,1:T(8,128)(2,1)} %param.28, f32[64,2560]{1,0:T(8,128)} %get-tuple-element.8, f32[2560]{0:T(1024)} %param.27), kind=kOutput, calls=%fused_computation.1 | convolution fusion | flops 63252480 | bytes 1566720 | tf_op jit(solution)/shard_map/dot_general | solution.py:125
  292.9 0.0 copy-done.1
  292.9 24.5 %psum.31 = f32[64,160]{1,0:T(8,128)S(1)} all-reduce(f32[64,160]{1,0:T(8,128)} %convolution_add_fusion), channel_id=1, replica_groups=mesh['gx'=32,'gy'=8] {'gy'}, use_global_device_ids=true, to_apply=%region_9.10 | all-reduce | flops 10240 | bytes 81920 | tf_op jit(solution)/shard_map/psum | solution.py:126
  317.4 0.0 copy-done.11
  317.4 0.0 copy-done.12
  317.4 0.6 fusion.57
  (13 shorter events, 0.2 us)
Async XLA Ops:
  7.2 77.2 %copy-start = (bf16[160,2560]{1,0:T(8,128)(2,1)S(1)}, bf16[160,2560]{1,0:T(8,128)(2,1)}, u32[]{:S(2)}) copy-start(bf16[160,2560]{1,0:T(8,128)(2,1)} %param.26) | copy-start | bytes 2457604
  7.2 1.8 copy-start.3
  7.2 229.3 %all-reduce.5.cloned.1.call-start = ((), (), s32[]{:S(2)}) async-start(), calls=%async_computation | async-start | bytes 2293760
  9.0 1.5 copy-start.4
  9.0 75.4 %copy-start.7 = (f32[160]{0:T(256)S(1)}, f32[160]{0:T(256)}, u32[]{:S(2)}) copy-start(f32[160]{0:T(256)} %param.21) | copy-start | bytes 1924
  9.0 75.4 %copy-start.8 = (f32[160]{0:T(256)S(1)}, f32[160]{0:T(256)}, u32[]{:S(2)}) copy-start(f32[160]{0:T(256)} %param.20) | copy-start | bytes 1924
  9.0 76.5 %copy-start.6 = (s32[64]{0:T(128)S(1)}, s32[64]{0:T(128)}, u32[]{:S(2)}) copy-start(s32[64]{0:T(128)} %param.33) | copy-start | bytes 772
  9.0 76.5 %copy-start.9 = (f32[160]{0:T(256)S(1)}, f32[160]{0:T(256)}, u32[]{:S(2)}) copy-start(f32[160]{0:T(256)} %param.19) | copy-start | bytes 1924
  9.0 76.5 %copy-start.10 = (f32[160]{0:T(256)S(1)}, f32[160]{0:T(256)}, u32[]{:S(2)}) copy-start(f32[160]{0:T(256)} %param.18) | copy-start | bytes 1924
  10.5 77.6 %copy-start.13 = (s32[64]{0:T(128)S(1)}, s32[64]{0:T(128)}, u32[]{:S(2)}) copy-start(s32[64]{0:T(128)} %param.32) | copy-start | bytes 772
  10.5 81.0 %copy-start.14 = (u32[256]{0:T(256)S(1)}, u32[256]{0:T(256)}, u32[]{:S(2)}) copy-start(u32[256]{0:T(256)} %constant.103) | copy-start | bytes 3076
  10.5 225.9 %copy-start.5 = (f32[1920]{0:T(1024)S(1)}, f32[1920]{0:T(1024)}, u32[]{:S(2)}) copy-start(f32[1920]{0:T(1024)} %param.23) | copy-start | bytes 23044
  85.5 157.8 %copy-start.2 = (bf16[2,5,1024,128]{3,2,1,0:T(8,128)(2,1)S(1)}, bf16[2,5,1024,128]{3,2,1,0:T(8,128)(2,1)}, u32[]{:S(2)}) copy-start(bf16[2,5,1024,128]{3,2,1,0:T(8,128)(2,1)} %param.31) | copy-start | bytes 7864324
  243.4 49.5 %copy-start.1 = (bf16[2,5,1024,128]{3,2,1,0:T(8,128)(2,1)}, bf16[2,5,1024,128]{3,2,1,0:T(8,128)(2,1)S(1)}, u32[]{:S(2)}) copy-start(bf16[2,5,1024,128]{3,2,1,0:T(8,128)(2,1)S(1)} %dynamic_update_slice.15) | copy-start | bytes 7864324
  289.3 28.1 %copy-start.11 = (f32[160]{0:T(256)S(1)}, f32[160]{0:T(256)}, u32[]{:S(2)}) copy-start(f32[160]{0:T(256)} %param.29) | copy-start | bytes 1924
  289.4 28.1 %copy-start.12 = (f32[160]{0:T(256)S(1)}, f32[160]{0:T(256)}, u32[]{:S(2)}) copy-start(f32[160]{0:T(256)} %param.25) | copy-start | bytes 1924
Sparse Core Ops, SparseCore 0:
  88.2 148.2 all-reduce.4
where the time goes:
time: 325 us
  waiting for transfers between devices  142 us (44%)
  blocking collectives  140 us (43%)
  between operations  18.9 us (6%)
  matrix products  12.2 us (4%)
  local copies, waits for them, and re-layouts  9.11 us (3%)
    unnamed x2, waiting for transfers between devices  142 us
    psum x1, blocking collectives, on_device(): lax.psum((jnp.sum(wide_in, axis=1), jnp.sum(wide_in * wide_in, axis=1)),...  73.7 us
    all_gather x1, blocking collectives, on_device(): lax.all_gather(attended, 'gx', axis=0, tiled=True)  41.8 us
    psum x1, blocking collectives, on_device(): branches = lax.psum(attn_part + mlp_part, 'gy')  24.5 us
  transfers between devices with their start and end apart: 1, of which 1 were waited for; matrix products, arithmetic and copies ran while one was open for 0% of the time, Pallas kernels for 0%

commit v1 on v0

--- a/solution.py
+++ b/solution.py
@@ -1,3 +1,4 @@
+import functools
 import jax
 import jax.numpy as jnp
 from jax import lax
@@ -6,6 +7,23 @@
 D = 5120
 HD = 128
 ROT = 32
+
+
+def raise_targets(mine_x, shard_axis, where_dim):
+    n_chips = lax.axis_size(shard_axis)
+    arrivals = []
+    for dev_j in range(mine_x.ndim):
+        arrivals.append(n_chips if dev_j == where_dim else 1)
+    return lax.all_to_all(
+        jnp.tile(mine_x, arrivals),
+        shard_axis,
+        split_axis=where_dim,
+        concat_axis=where_dim,
+        tiled=True,
+    )
+
+
+unite_classes_all = functools.partial(raise_targets, shard_axis="gx", where_dim=0)
 
 
 def rotate(tensor, position):
@@ -113,11 +131,7 @@
         "shp,shpd->shd", weights_low, new_values, preferred_element_type=jnp.float32
     )
     attended = (weighted / total[:, :, None]).astype(jnp.bfloat16).reshape(rows_dev, heads_dev * HD)
-    slot_part = jnp.dot(
-        lax.all_gather(attended, "gx", axis=0, tiled=True),
-        w_out,
-        preferred_element_type=jnp.float32,
-    )
+    slot_part = jnp.dot(unite_classes_all(attended), w_out, preferred_element_type=jnp.float32)
     attn_part = jnp.dot(to_request, slot_part, precision=lax.Precision.HIGHEST)
     up_partial = jnp.dot(mlp_in, w_up, preferred_element_type=jnp.float32)
     up = lax.psum(up_partial, "gx") + b_up

time: 325 us -> 299 us (0.920)
  blocking collectives: 140 us -> 114 us
    all_gather x1 -> x0, blocking collectives: 41.8 us -> none  [on_device(): lax.all_gather(attended, 'gx', axis=0, tiled=True)]
    all_to_all x0 -> x1, blocking collectives: none -> 16 us  [raise_targets(): lax.all_to_all(jnp.tile(mine_x, arrivals), shard_axis, split_axis=where_d...]
  transfers between devices with their start and end apart: 1 -> 1, of which waited for: 1 -> 1; matrix products, arithmetic and copies ran while one was open for 0% -> 1% of each run, Pallas kernels for 0% -> 0%
where the time goes in v1:
time: 299 us; the launch traced here: 298 us
  waiting for transfers between devices  142 us (47%)
  blocking collectives  114 us (38%)
  between operations  18.9 us (6%)
  matrix products  12.2 us (4%)
  local copies, waits for them, and re-layouts  8.26 us (3%)
    unnamed x2, waiting for transfers between devices  142 us
    psum x1, blocking collectives, on_device(): lax.psum((jnp.sum(wide_in, axis=1), jnp.sum(wide_in * wide_in, axis=1)),...  73.7 us
    psum x1, blocking collectives, on_device(): branches = lax.psum(attn_part + mlp_part, 'gy')  24.5 us
    all_to_all x1, blocking collectives, raise_targets(): lax.all_to_all(jnp.tile(mine_x, arrivals), shard_axis, split_axis=where_d...  16 us
  transfers between devices with their start and end apart: 1, of which 1 were waited for; matrix products, arithmetic and copies ran while one was open for 1% of the time, Pallas kernels for 0%

profile of v1, /device:TPU:2, one launch (start us, length us, event | category | flops | bytes accessed | tf_op | source)
XLA Modules:
  0.0 298.2 jit_solution(8507129718702844701)
XLA Ops:
  7.2 0.0 copy-start
  7.2 0.0 copy-start.3
  7.2 0.0 all-reduce.5.cloned.1.call-start
  7.2 1.8 copy-done.3
  9.0 0.0 copy-start.4
  9.0 0.0 copy-start.7
  9.0 0.0 copy-start.8
  9.0 0.0 copy-start.6
  9.0 0.0 copy-start.9
  9.0 0.0 copy-start.10
  9.0 1.5 copy.71
  10.5 0.0 copy-done.4
  10.5 0.0 copy-start.13
  10.5 0.0 copy-start.14
  10.5 0.1 convert_reduce_fusion
  10.7 73.7 %all-reduce.1 = (f32[64]{0:T(128)S(1)}, f32[64]{0:T(128)S(1)}) all-reduce(f32[64]{0:T(128)S(1)} %get-tuple-element.4, f32[64]{0:T(128)S(1)} %get-tuple-element.3), channel_id=1, replica_groups=mesh['gx'=32,'gy'=8] {'gx'}, use_global_device_ids=true, to_apply=%region_4.5 | all-reduce | flops 128 | bytes 1024 | tf_op jit(solution)/shard_map/psum | solution.py:80
  84.4 0.0 copy-done
  84.4 0.0 copy-done.7
  84.4 0.0 copy-done.8
  84.4 1.2 fusion.61
  85.5 0.0 copy-done.6
  85.5 0.0 copy-done.9
  85.5 0.0 copy-done.10
  85.5 2.5 fusion.4
  88.0 0.0 all-reduce.5.cloned.1.call-update
  88.1 0.0 copy-done.13
  88.1 0.1 select_reduce_fusion
  88.2 0.1 broadcast_add_fusion
  88.3 0.6 fusion.122
  91.5 0.0 copy-done.14
  91.5 0.6 dynamic-slice
  94.1 0.1 multiply_cosine_fusion
  94.2 0.1 iota_compare_fusion.4
  94.3 142.2 %all-reduce.5.cloned.1.call-done = (f32[64,1920]{1,0:T(8,128)}, f32[64,2560]{1,0:T(8,128)}) async-done(((f32[64,1920]{1,0:T(8,128)}, f32[64,2560]{1,0:T(8,128)}), (f32[64,1920]{1,0:T(8,128)}, f32[64,2560]{1,0:T(8,128)})) %all-reduce.5.cloned.1.call-update) | async-done | bytes 1146896
  236.5 0.0 copy-done.5
  236.5 0.8 dynamic-slice_add_fusion
  237.4 0.1 slice.91
  237.5 0.1 slice.90
  237.5 0.1 subtract_convert_fusion.1
  237.6 0.1 pad_maximum_fusion
  237.7 0.1 maximum_bitcast_fusion
  237.8 1.3 dynamic_update_slice.12
  239.1 1.3 dynamic_update_slice.13
  240.5 2.5 fusion.84
  243.0 0.1 fusion.3
  243.1 0.1 convert_bitcast_fusion
  243.2 0.1 copy.42
  243.3 0.0 copy-done.2
  243.4 0.0 copy-start.1
  243.4 0.4 fusion.59
  243.8 0.1 fusion.86
  243.9 0.1 tile.9
  244.0 16.0 %all_to_all.9 = bf16[32,2,640]{2,1,0:T(2,128)(2,1)S(1)} all-to-all(bf16[32,2,640]{2,1,0:T(2,128)(2,1)S(1)} %tile.9), channel_id=1, replica_groups=mesh['gx'=32,'gy'=8] {'gx'}, dimensions={0} | all-to-all | bytes 163840 | tf_op jit(solution)/shard_map/all_to_all | solution.py:17
  259.9 0.7 all_to_all.7
  260.6 1.2 fusion.123
  261.8 0.9 fusion.77
  262.7 0.0 copy-start.11
  262.7 0.0 copy-start.12
  262.7 3.5 %convolution_add_fusion = f32[64,160]{1,0:T(8,128)} fusion(f32[64,160]{1,0:T(8,128)S(1)} %fusion.77, bf16[2560,160]{0,1:T(8,128)(2,1)} %param.28, f32[64,2560]{1,0:T(8,128)} %get-tuple-element.8, f32[2560]{0:T(1024)} %param.27), kind=kOutput, calls=%fused_computation.1 | convolution fusion | flops 63252480 | bytes 1566720 | tf_op jit(solution)/shard_map/dot_general | solution.py:139
  266.3 0.0 copy-done.1
  266.3 24.5 %psum.31 = f32[64,160]{1,0:T(8,128)S(1)} all-reduce(f32[64,160]{1,0:T(8,128)} %convolution_add_fusion), channel_id=1, replica_groups=mesh['gx'=32,'gy'=8] {'gy'}, use_global_device_ids=true, to_apply=%region_9.10 | all-reduce | flops 10240 | bytes 81920 | tf_op jit(solution)/shard_map/psum | solution.py:140
  290.7 0.0 copy-done.11
  290.8 0.0 copy-done.12
  290.8 0.6 fusion.57
  (14 shorter events, 0.2 us)
Async XLA Ops:
  7.2 77.2 %copy-start = (bf16[160,2560]{1,0:T(8,128)(2,1)S(1)}, bf16[160,2560]{1,0:T(8,128)(2,1)}, u32[]{:S(2)}) copy-start(bf16[160,2560]{1,0:T(8,128)(2,1)} %param.26) | copy-start | bytes 2457604
  7.2 1.8 copy-start.3
  7.2 229.3 %all-reduce.5.cloned.1.call-start = ((), (), s32[]{:S(2)}) async-start(), calls=%async_computation.1 | async-start | bytes 2293760
  9.0 1.5 copy-start.4
  9.0 75.4 %copy-start.7 = (f32[160]{0:T(256)S(1)}, f32[160]{0:T(256)}, u32[]{:S(2)}) copy-start(f32[160]{0:T(256)} %param.21) | copy-start | bytes 1924
  9.0 75.4 %copy-start.8 = (f32[160]{0:T(256)S(1)}, f32[160]{0:T(256)}, u32[]{:S(2)}) copy-start(f32[160]{0:T(256)} %param.20) | copy-start | bytes 1924
  9.0 76.5 %copy-start.6 = (s32[64]{0:T(128)S(1)}, s32[64]{0:T(128)}, u32[]{:S(2)}) copy-start(s32[64]{0:T(128)} %param.33) | copy-start | bytes 772
  9.0 76.5 %copy-start.9 = (f32[160]{0:T(256)S(1)}, f32[160]{0:T(256)}, u32[]{:S(2)}) copy-start(f32[160]{0:T(256)} %param.19) | copy-start | bytes 1924
  9.0 76.5 %copy-start.10 = (f32[160]{0:T(256)S(1)}, f32[160]{0:T(256)}, u32[]{:S(2)}) copy-start(f32[160]{0:T(256)} %param.18) | copy-start | bytes 1924
  10.5 77.6 %copy-start.13 = (s32[64]{0:T(128)S(1)}, s32[64]{0:T(128)}, u32[]{:S(2)}) copy-start(s32[64]{0:T(128)} %param.32) | copy-start | bytes 772
  10.5 81.0 %copy-start.14 = (u32[256]{0:T(256)S(1)}, u32[256]{0:T(256)}, u32[]{:S(2)}) copy-start(u32[256]{0:T(256)} %constant.103) | copy-start | bytes 3076
  10.5 225.9 %copy-start.5 = (f32[1920]{0:T(1024)S(1)}, f32[1920]{0:T(1024)}, u32[]{:S(2)}) copy-start(f32[1920]{0:T(1024)} %param.23) | copy-start | bytes 23044
  85.5 157.8 %copy-start.2 = (bf16[2,5,1024,128]{3,2,1,0:T(8,128)(2,1)S(1)}, bf16[2,5,1024,128]{3,2,1,0:T(8,128)(2,1)}, u32[]{:S(2)}) copy-start(bf16[2,5,1024,128]{3,2,1,0:T(8,128)(2,1)} %param.31) | copy-start | bytes 7864324
  243.4 22.9 %copy-start.1 = (bf16[2,5,1024,128]{3,2,1,0:T(8,128)(2,1)}, bf16[2,5,1024,128]{3,2,1,0:T(8,128)(2,1)S(1)}, u32[]{:S(2)}) copy-start(bf16[2,5,1024,128]{3,2,1,0:T(8,128)(2,1)S(1)} %dynamic_update_slice.15) | copy-start | bytes 7864324
  262.7 28.1 %copy-start.11 = (f32[160]{0:T(256)S(1)}, f32[160]{0:T(256)}, u32[]{:S(2)}) copy-start(f32[160]{0:T(256)} %param.29) | copy-start | bytes 1924
  262.7 28.1 %copy-start.12 = (f32[160]{0:T(256)S(1)}, f32[160]{0:T(256)}, u32[]{:S(2)}) copy-start(f32[160]{0:T(256)} %param.25) | copy-start | bytes 1924
Sparse Core Ops, SparseCore 0:
  88.2 148.2 all-reduce.4
